TPU v7x, 256 devices: a whole 4x4x8 slice. The times are simulated.
256 devices in a mesh: req: 2 (over core), seq: 16 (over y, x), tp: 8 (over z).
Axes of the slice: x: 4, y: 4, z: 8, core: 2. Of those that a mesh axis runs over, the one named last changes fastest.
Arguments:
- queries: bfloat16 [4, 512, 3072], P('req', 'seq', 'tp'), may hold values from -48 to 48
- new_kv: bfloat16 [4, 512, 2, 3072], P('req', 'seq', None, 'tp'), may hold values from -4 to 4
- cache_kv: bfloat16 [4, 16384, 2, 3072], P('req', 'seq', None, 'tp'), may hold values from -4 to 4
- cached_len: int32 [4], P('req'), may hold values from 1 to 16384, as said below
- residual_in: bfloat16 [4, 512, 3072], P('req', 'seq', 'tp'), may hold values from -1.5 to 1.5
- norm_gain: float32 [3072], replicated, may hold values from 0.1 to 1.9
- gate_w: bfloat16 [3072, 4096], P(None, 'tp'), may hold values from -0.109375 to 0.109375
- up_w: bfloat16 [3072, 4096], P(None, 'tp'), may hold values from -0.109375 to 0.109375
- down_w: bfloat16 [4096, 3072], P('tp'), may hold values from -0.09375 to 0.09375
- owner: int32 [32, 64, 1], P(('req', 'seq')), may hold values from 0 to 31; in each aligned block of 64 rows (0 to 63, 64 to 127, ..., all dimensions but the last counted through in order) at most 4 rows name the same one
Outputs:
- layer_out: bfloat16 [32, 32, 4, 3072], P(('req', 'seq'), None, None, 'tp')
Inputs may be any that keep to these rules, and one draw needn't show every extreme that they name: `cached_len`: exactly 1 request have 16384 - 16384 // 8 cached positions or more, one of them exactly 16384; every other request has at most 1024. Within one row block no owner is named by more than 4 rows.
All inputs are finite; a program needn't handle non-finite values.
Results may differ from a plain program's by a relative error of at most 0.02.
Values may be sent and summed in bfloat16 or wider, within the bound.
No kernel may reach another device: no remote copies, remote signals or barrier semaphores. Data moves between devices by JAX's collectives and lax.ppermute only.
A program may use at most 256 MiB of HBM per device.

v0:
```python
import jax
import jax.numpy as jnp
from jax import lax
from jax.sharding import PartitionSpec as P

HEAD = 96
masked_floor = -1e30


def block_stats(query_heads, key_heads, value_heads, visible):
    scores = jnp.einsum(
        "qhd,khd->qhk", query_heads, key_heads, preferred_element_type=jnp.float32
    ) * HEAD ** (-0.5)
    visible_heads = visible[:, None, :]
    masked = jnp.where(visible_heads, scores, masked_floor)
    row_peak = jnp.max(masked, axis=-1)
    weights = jnp.where(visible_heads, jnp.exp(masked - row_peak[..., None]), 0.0)
    row_total = jnp.sum(weights, axis=-1)
    weighted = jnp.einsum(
        "qhk,khd->qhd",
        weights.astype(jnp.bfloat16),
        value_heads,
        preferred_element_type=jnp.float32,
    )
    return (row_peak, row_total, weighted.reshape(weighted.shape[0], -1))


def slot_partial(query_slot, cached_slot, fresh_slot, length, seq_index):
    query_count = query_slot.shape[0]
    head_count = query_slot.shape[1] // HEAD
    query_heads = query_slot.reshape(query_count, head_count, HEAD)
    positions = jnp.arange(query_count, dtype=jnp.int32)
    fresh_count = fresh_slot.shape[0]
    fresh_index = seq_index * fresh_count + jnp.arange(fresh_count, dtype=jnp.int32)
    fresh_visible = fresh_index[None, :] <= positions[:, None]
    shard_span = cached_slot.shape[0]
    shard_offset = seq_index * shard_span
    key_total = shard_span + fresh_count
    keys_all = jnp.concatenate([cached_slot[:, 0], fresh_slot[:, 0]], axis=0).reshape(
        key_total, head_count, HEAD
    )
    values_all = jnp.concatenate([cached_slot[:, 1], fresh_slot[:, 1]], axis=0).reshape(
        key_total, head_count, HEAD
    )
    cached_index = shard_offset + jnp.arange(shard_span, dtype=jnp.int32)
    cached_visible = jnp.broadcast_to((cached_index < length)[None, :], (query_count, shard_span))
    visible = jnp.concatenate([cached_visible, fresh_visible], axis=1)
    return block_stats(query_heads, keys_all, values_all, visible)


def normalize(features, norm_gain):
    values = features.astype(jnp.float32)
    mean_square = jnp.mean(values * values, axis=-1, keepdims=True)
    return (values * lax.rsqrt(mean_square + 1e-05) * norm_gain).astype(jnp.bfloat16)


def per_device(
    queries, new_kv, cache_kv, cached_len, residual_in, norm_gain, gate_w, up_w, down_w, owner
):
    slot_count, token_count, width_local = queries.shape
    seq_index = lax.axis_index("seq")
    all_queries = lax.all_gather(queries, "seq", axis=1, tiled=True)
    partials = [
        slot_partial(
            all_queries[slot_number],
            cache_kv[slot_number],
            new_kv[slot_number],
            cached_len[slot_number],
            seq_index,
        )
        for slot_number in range(slot_count)
    ]
    row_peak = jnp.stack([partial_item[0] for partial_item in partials])
    row_total = jnp.stack([partial_item[1] for partial_item in partials])
    weighted = jnp.stack([partial_item[2] for partial_item in partials])
    pieces = (
        lax.all_to_all(row_peak[None], "seq", split_axis=2, concat_axis=0, tiled=True),
        lax.all_to_all(row_total[None], "seq", split_axis=2, concat_axis=0, tiled=True),
        lax.all_to_all(weighted[None], "seq", split_axis=2, concat_axis=0, tiled=True),
    )
    source_peak, source_total, source_sum = pieces
    joint_peak = jnp.max(source_peak, axis=0)
    source_scale = jnp.exp(source_peak - joint_peak[None])
    own_total = jnp.sum(source_total * source_scale, axis=0)
    grouped = source_sum.reshape(source_sum.shape[:-1] + (source_peak.shape[-1], HEAD))
    own_sum = jnp.sum(grouped * source_scale[..., None], axis=0).reshape(source_sum.shape[1:])
    head_count = width_local // HEAD
    attention = (
        own_sum.reshape(slot_count, token_count, head_count, HEAD) / own_total[..., None]
    ).reshape(slot_count, token_count, width_local)
    stream = (residual_in.astype(jnp.float32) + attention).astype(jnp.bfloat16)
    stream_rows = stream.reshape(slot_count * token_count, width_local)
    owner_ids = owner.reshape(-1)
    owner_count = lax.axis_size(("req", "seq"))
    row_count = owner_ids.shape[0]
    slot_cap = max(2, 2 * row_count // owner_count)
    matches = (owner_ids[:, None] == jnp.arange(owner_count, dtype=jnp.int32)[None, :]).astype(
        jnp.int32
    )
    ranking = jnp.sum(jnp.cumsum(matches, axis=0) * matches, axis=1) - 1
    outgoing = (
        jnp.zeros((owner_count * slot_cap, width_local), jnp.bfloat16)
        .at[owner_ids * slot_cap + ranking]
        .set(stream_rows)
    )
    incoming = lax.all_to_all(
        outgoing.reshape(owner_count, slot_cap, width_local),
        ("req", "seq"),
        split_axis=0,
        concat_axis=0,
        tiled=True,
    )
    arrived = incoming.reshape(owner_count * slot_cap, width_local)
    full_rows = lax.all_gather(arrived, "tp", axis=1, tiled=True)
    normed = normalize(full_rows, norm_gain)
    gate_out = jnp.dot(normed, gate_w, preferred_element_type=jnp.float32)
    up_out = jnp.dot(normed, up_w, preferred_element_type=jnp.float32)
    hidden = (jax.nn.silu(gate_out) * up_out).astype(jnp.bfloat16)
    partial_sum = jnp.dot(hidden, down_w, preferred_element_type=jnp.float32)
    unit_share = lax.psum_scatter(
        partial_sum.astype(jnp.bfloat16), "tp", scatter_dimension=1, tiled=True
    ).astype(jnp.float32)
    result = (arrived.astype(jnp.float32) + unit_share).astype(jnp.bfloat16)
    return result.reshape(1, owner_count, slot_cap, width_local)


def solution(mesh):
    return jax.shard_map(
        per_device,
        mesh=mesh,
        in_specs=(
            P("req", "seq", "tp"),
            P("req", "seq", None, "tp"),
            P("req", "seq", None, "tp"),
            P("req"),
            P("req", "seq", "tp"),
            P(),
            P(None, "tp"),
            P(None, "tp"),
            P("tp", None),
            P(("req", "seq"), None, None),
        ),
        out_specs=P(("req", "seq"), None, None, "tp"),
        check_vma=False,
    )
```

profile of v0, /device:TPU:2, one launch (start us, length us, event | category | flops | bytes accessed | tf_op | source)
XLA Modules:
  0.0 262.6 jit_solution(4247062035156930165)
XLA Ops:
  6.5 1.4 fusion.65
  8.0 1.3 fusion.45
  10.5 0.9 slice_bitcast_fusion.3
  13.7 24.4 %all_gather.6 = bf16[2,512,384]{2,1,0:T(8,128)(2,1)S(1)} all-gather(bf16[2,32,384]{2,1,0:T(8,128)(2,1)} %param.10), channel_id=1, replica_groups=mesh['req'=2,'seq'=16,'tp'=8] {'seq'}, dimensions={1}, use_global_device_ids=true | all-gather | bytes 835584 | tf_op jit(solution)/shard_map/all_gather | solution.py:62
  38.9 1.9 copy.57
  40.8 0.9 copy.62
  41.8 3.9 %slice_bitcast_fusion.1 = (bf16[1024,2,384]{2,1,0:T(2,128)(2,1)S(1)}, bf16[1024,2,384]{2,1,0:T(2,128)(2,1)S(1)}) fusion(bf16[2,1024,2,384]{3,2,1,0:T(2,128)(2,1)} %param.12), kind=kLoop, calls=%fused_computation.26 | loop fusion | bytes 6291456 | tf_op jit(solution)/shard_map/squeeze | solution.py:66
  45.6 6.3 %fusion.60 = (bf16[1024,1,384]{2,1,0:T(2,128)(2,1)}, bf16[1024,1,384]{2,1,0:T(2,128)(2,1)}, bf16[1024,1,384]{2,1,0:T(2,128)(2,1)}, bf16[1024,1,384]{2,1,0:T(2,128)(2,1)}) fusion(bf16[1024,2,384]{2,1,0:T(2,128)(2,1)S(1)} %get-tuple-element.7, bf16[1024,2,384]{2,1,0:T(2,128)(2,1)S(1)} %get-tuple-element.8), kind=kLoop, calls=%fused_computation.86 | loop fusion | bytes 6291456 | tf_op jit(solution)/shard_map/slice | solution.py:42
  51.9 4.7 %copy.55 = bf16[1024,1,384]{0,2,1:T(8,128)(2,1)} copy(bf16[1024,1,384]{2,1,0:T(2,128)(2,1)} %get-tuple-element.10) | data formatting | bytes 1572864 | tf_op jit(solution)/shard_map/slice | solution.py:39
  56.6 4.7 %copy.60 = bf16[1024,1,384]{0,2,1:T(8,128)(2,1)} copy(bf16[1024,1,384]{2,1,0:T(2,128)(2,1)} %get-tuple-element.33) | data formatting | bytes 1572864 | tf_op jit(solution)/shard_map/slice | solution.py:39
  61.3 1.8 pad_add_fusion.1
  63.2 6.7 %fusion.1 = (f32[512,4]{0,1:T(4,128)S(1)}, f32[4,1056,512]{2,1,0:T(8,128)}) fusion(pred[512,1056]{0,1:T(8,128)(4,1)S(1)} %get-tuple-element.22, bf16[512,4,96]{0,2,1:T(8,128)(2,1)S(1)} %bitcast.116, bf16[32,4,96]{0,2,1:T(8,128)(2,1)} %bitcast.118, bf16[1024,4,96]{0,2,1:T(8,128)(2,1)} %bitcast.114), kind=kOutput, calls=%fused_computation.6 | convolution fusion | flops 423344128 | bytes 10403840 | tf_op jit(solution)/shard_map/qhd,khd->qhk/dot_general | solution.py:11
  69.9 5.2 %fusion = (f32[512,4]{0,1:T(4,128)S(1)}, f32[4,1056,512]{2,1,0:T(8,128)}) fusion(pred[512,1056]{0,1:T(8,128)(4,1)S(1)} %get-tuple-element.21, bf16[512,4,96]{0,2,1:T(8,128)(2,1)S(1)} %bitcast.115, bf16[32,4,96]{0,2,1:T(8,128)(2,1)S(1)} %bitcast.117, bf16[1024,4,96]{0,2,1:T(8,128)(2,1)S(1)} %bitcast.112), kind=kOutput, calls=%fused_computation.5 | convolution fusion | flops 423344128 | bytes 10403840 | tf_op jit(solution)/shard_map/qhd,khd->qhk/dot_general | solution.py:11
  75.1 1.0 copy.66
  76.1 1.9 bitcast_bitcast_fusion.1
  78.0 2.4 reshape.128
  80.3 5.7 %all-to-all-start.1 = ((f32[16,1,256]{2,1,0:T(1,128)}), f32[16,1,256]{2,1,0:T(1,128)S(1)}, u32[]{:S(2)}, u32[]{:S(2)}) async-start(f32[16,1,256]{2,1,0:T(1,128)} %reshape.128), calls=%async_computation.1 | async-start | bytes 32768 | tf_op jit(solution)/shard_map/all_to_all | solution.py:77
  86.9 4.7 %copy.53 = bf16[1024,1,384]{0,2,1:T(8,128)(2,1)} copy(bf16[1024,1,384]{2,1,0:T(2,128)(2,1)} %get-tuple-element.9) | data formatting | bytes 1572864 | tf_op jit(solution)/shard_map/slice | solution.py:42
  91.6 4.7 %copy.58 = bf16[1024,1,384]{0,2,1:T(8,128)(2,1)} copy(bf16[1024,1,384]{2,1,0:T(2,128)(2,1)} %get-tuple-element.34) | data formatting | bytes 1572864 | tf_op jit(solution)/shard_map/slice | solution.py:42
  96.3 4.8 %fusion.4 = f32[512,4]{0,1:T(4,128)S(1)} fusion(f32[4,1056,512]{2,1,0:T(8,128)} %get-tuple-element.26, f32[512,4]{0,1:T(4,128)S(1)} %get-tuple-element.25, pred[512,1056]{0,1:T(8,128)(4,1)} %copy-done.7), kind=kLoop, calls=%fused_computation.9 | loop fusion | flops 10811392 | bytes 9207808 | tf_op jit(solution)/shard_map/reduce_sum | solution.py:18
  101.1 1.3 copy-done.1
  102.5 2.2 fusion.2
  104.7 1.0 copy.69
  105.7 7.5 %fusion.6 = f32[4,96,512]{2,1,0:T(8,128)} fusion(f32[4,1056,512]{2,1,0:T(8,128)} %get-tuple-element.26, f32[512,4]{0,1:T(4,128)S(1)} %get-tuple-element.25, pred[512,1056]{0,1:T(8,128)(4,1)} %copy-done.7, bf16[32,4,96]{0,2,1:T(8,128)(2,1)} %bitcast.120, bf16[1024,4,96]{0,2,1:T(8,128)(2,1)} %bitcast.113), kind=kOutput, calls=%fused_computation.11 | convolution fusion | flops 427671552 | bytes 10797056 | tf_op jit(solution)/shard_map/qhk,khd->qhd/dot_general | solution.py:19
  113.3 3.7 %fusion.8 = f32[4,96,512]{2,1,0:T(8,128)} fusion(f32[4,1056,512]{2,1,0:T(8,128)S(1)} %bitcast.104, f32[512,4]{0,1:T(4,128)S(1)} %get-tuple-element.27, pred[512,1056]{0,1:T(8,128)(4,1)S(1)} %copy-done.6, bf16[32,4,96]{0,2,1:T(8,128)(2,1)S(1)} %bitcast.119, bf16[1024,4,96]{0,2,1:T(8,128)(2,1)S(1)} %bitcast.111), kind=kOutput, calls=%fused_computation.12 | convolution fusion | flops 427671552 | bytes 10797056 | tf_op jit(solution)/shard_map/qhk,khd->qhd/dot_general | solution.py:19
  117.8 3.1 %copy.64 = f32[1,512,384]{2,0,1:T(1,128)} copy(f32[1,512,384]{1,2,0:T(8,128)} %bitcast.109) | data formatting | bytes 1572864 | tf_op jit(solution)/shard_map/stack;reshape | solution.py:75
  120.9 3.0 %copy.63 = f32[1,512,384]{2,0,1:T(1,128)} copy(f32[1,512,384]{1,2,0:T(8,128)} %bitcast.110) | data formatting | bytes 1572864 | tf_op jit(solution)/shard_map/stack;reshape | solution.py:75
  123.9 2.4 reshape.130
  126.3 7.2 %all-to-all-start.2 = ((f32[16,1,256]{2,1,0:T(1,128)}), f32[16,1,256]{2,1,0:T(1,128)S(1)}, u32[]{:S(2)}, u32[]{:S(2)}) async-start(f32[16,1,256]{2,1,0:T(1,128)} %reshape.130), calls=%async_computation.2 | async-start | bytes 32768 | tf_op jit(solution)/shard_map/all_to_all | solution.py:78
  133.5 3.9 %maximum_bitcast_fusion = f32[1,2,512,384]{3,1,0,2:T(2,128)} fusion(f32[1,512,384]{2,0,1:T(1,128)} %copy.64, f32[1,512,384]{2,0,1:T(1,128)} %copy.63), kind=kLoop, calls=%fused_computation.23 | loop fusion | flops 393216 | bytes 3145728 | tf_op jit(solution)/shard_map/broadcast_in_dim | solution.py:79
  137.4 2.3 all-to-all-done.2
  139.7 5.6 %all-to-all-start = ((f32[1,2,512,384]{3,1,0,2:T(2,128)}), f32[1,2,512,384]{3,1,0,2:T(2,128)}, u32[]{:S(2)}, u32[]{:S(2)}) async-start(f32[1,2,512,384]{3,1,0,2:T(2,128)} %maximum_bitcast_fusion), calls=%async_computation | async-start | bytes 3145728 | tf_op jit(solution)/shard_map/all_to_all | solution.py:79
  147.2 1.6 reshape.129
  148.8 1.3 copy.67
  150.8 1.6 reshape.131
  152.4 1.3 copy.70
  154.2 1.1 copy.68
  155.2 3.2 %mul.89 = f32[16,2,32,4,96]{4,3,2,0,1:T(4,128)} broadcast(f32[16,2,32,4]{3,2,0,1:T(8,128)} %copy.68), dimensions={0,1,2,3} | broadcast | bytes 1589248 | tf_op jit(solution)/shard_map/mul | solution.py:86
  158.4 3.2 %mul.90 = f32[16,1,2,32,384]{4,3,0,2,1:T(8,128)} reshape(f32[16,2,32,4,96]{4,3,2,0,1:T(4,128)} %mul.89) | data formatting | bytes 3145728 | tf_op jit(solution)/shard_map/mul | solution.py:86
  161.6 1.6 copy.65
  163.8 0.9 scatter_custom_fusion
  164.7 13.5 %all_to_all.56 = bf16[32,4,384]{2,1,0:T(4,128)(2,1)S(1)} all-to-all(bf16[32,4,384]{2,1,0:T(4,128)(2,1)S(1)} %reshape.111), channel_id=1, replica_groups=mesh['req'=2,'seq'=16,'tp'=8] {'req','seq'}, dimensions={0} | all-to-all | bytes 196608 | tf_op jit(solution)/shard_map/all_to_all | solution.py:106
  178.3 30.0 %all_gather.7 = bf16[128,3072]{1,0:T(8,128)(2,1)S(1)} all-gather(bf16[128,384]{1,0:T(8,128)(2,1)S(1)} %reshape.112), channel_id=1, replica_groups=mesh['req'=2,'seq'=16,'tp'=8] {'tp'}, dimensions={1}, use_global_device_ids=true | all-gather | bytes 884736 | tf_op jit(solution)/shard_map/all_gather | solution.py:114
  209.2 3.2 %fusion.37 = f32[128,512]{1,0:T(8,128)} fusion(bf16[3072,512]{1,0:T(8,128)(2,1)} %param.16, bf16[128,3072]{1,0:T(8,128)(2,1)S(1)} %all_gather.7, f32[3072]{0:T(1024)S(1)} %copy-done.18, f32[128]{0:T(128)S(1)} %add_rsqrt_fusion), kind=kOutput, calls=%fused_computation.48 | convolution fusion | flops 404226048 | bytes 4207104 | tf_op jit(solution)/shard_map/dot_general | solution.py:116
  212.4 4.2 %convolution_convert_fusion = bf16[128,3072]{1,0:T(8,128)(2,1)} fusion(bf16[512,3072]{1,0:T(8,128)(2,1)S(1)} %copy-done, bf16[3072,512]{1,0:T(8,128)(2,1)} %param.17, f32[128,512]{1,0:T(8,128)} %fusion.37, bf16[128,3072]{1,0:T(8,128)(2,1)} %copy-done.3, f32[3072]{0:T(1024)S(1)} %copy-done.18, f32[128]{0:T(128)S(1)} %add_rsqrt_fusion), kind=kOutput, calls=%fused_computation.15 | convolution fusion | flops 807665664 | bytes 8139264 | tf_op jit(solution)/shard_map/dot_general | solution.py:119
  216.6 2.3 copy.72
  218.9 35.1 %reduce-scatter.4.cloned.1.call-done = bf16[384,128]{1,0:T(8,128)(2,1)} async-done(((bf16[3072,128]{1,0:T(8,128)(2,1)}), bf16[384,128]{1,0:T(8,128)(2,1)}) %reduce-scatter.4.cloned.1.call-update) | async-done | bytes 98320
  254.1 1.0 copy.73
  (81 shorter events, 11.4 us)
Async XLA Ops:
  6.5 205.9 %copy-start = (bf16[512,3072]{1,0:T(8,128)(2,1)S(1)}, bf16[512,3072]{1,0:T(8,128)(2,1)}, u32[]{:S(2)}) copy-start(bf16[512,3072]{1,0:T(8,128)(2,1)} %param.18) | copy-start | bytes 9437188
  51.9 11.2 %copy-start.12 = (bf16[1,512,384]{1,2,0:T(8,128)(2,1)S(1)}, bf16[1,512,384]{1,2,0:T(8,128)(2,1)}, u32[]{:S(2)}) copy-start(bf16[1,512,384]{1,2,0:T(8,128)(2,1)} %copy.62) | copy-start | bytes 1179652
  63.1 6.8 %copy-start.7 = (pred[512,1056]{0,1:T(8,128)(4,1)}, pred[512,1056]{0,1:T(8,128)(4,1)S(1)}, u32[]{:S(2)}) copy-start(pred[512,1056]{0,1:T(8,128)(4,1)S(1)} %get-tuple-element.22) | copy-start | bytes 1622020
  63.1 6.8 %copy-start.4 = (pred[512,1056]{0,1:T(8,128)(4,1)}, pred[512,1056]{0,1:T(8,128)(4,1)S(1)}, u32[]{:S(2)}) copy-start(pred[512,1056]{0,1:T(8,128)(4,1)S(1)} %get-tuple-element.21) | copy-start | bytes 1622020
  63.1 6.7 %copy-start.10 = (bf16[1024,1,384]{0,2,1:T(8,128)(2,1)S(1)}, bf16[1024,1,384]{0,2,1:T(8,128)(2,1)}, u32[]{:S(2)}) copy-start(bf16[1024,1,384]{0,2,1:T(8,128)(2,1)} %copy.55) | copy-start | bytes 2359300
  63.1 6.7 %copy-start.11 = (bf16[1,512,384]{1,2,0:T(8,128)(2,1)S(1)}, bf16[1,512,384]{1,2,0:T(8,128)(2,1)}, u32[]{:S(2)}) copy-start(bf16[1,512,384]{1,2,0:T(8,128)(2,1)} %copy.57) | copy-start | bytes 1179652
  63.1 6.7 %copy-start.15 = (bf16[32,1,384]{0,2,1:T(8,128)(2,1)S(1)}, bf16[32,1,384]{0,2,1:T(8,128)(2,1)}, u32[]{:S(2)}) copy-start(bf16[32,1,384]{0,2,1:T(8,128)(2,1)} %copy.56) | copy-start | bytes 73732
  69.9 16.1 %copy-start.14 = (bf16[32,1,384]{2,1,0:T(2,128)(2,1)S(1)}, bf16[32,1,384]{2,1,0:T(2,128)(2,1)}, u32[]{:S(2)}) copy-start(bf16[32,1,384]{2,1,0:T(2,128)(2,1)} %get-tuple-element.17) | copy-start | bytes 73732
  69.9 16.3 %copy-start.13 = (bf16[32,1,384]{2,1,0:T(2,128)(2,1)S(1)}, bf16[32,1,384]{2,1,0:T(2,128)(2,1)}, u32[]{:S(2)}) copy-start(bf16[32,1,384]{2,1,0:T(2,128)(2,1)} %get-tuple-element.32) | copy-start | bytes 73732
  80.3 45.9 %all-to-all-start.1 = ((f32[16,1,256]{2,1,0:T(1,128)}), f32[16,1,256]{2,1,0:T(1,128)S(1)}, u32[]{:S(2)}, u32[]{:S(2)}) async-start(f32[16,1,256]{2,1,0:T(1,128)} %reshape.128), calls=%async_computation.1 | async-start | bytes 32768 | tf_op jit(solution)/shard_map/all_to_all | solution.py:77
  96.3 6.1 %copy-start.1 = (f32[4,1056,512]{2,1,0:T(8,128)S(1)}, f32[4,1056,512]{2,1,0:T(8,128)}, u32[]{:S(2)}) copy-start(f32[4,1056,512]{2,1,0:T(8,128)} %get-tuple-element.28) | copy-start | bytes 25952260
  96.3 6.2 %copy-start.5 = (pred[512,1056]{0,1:T(8,128)(4,1)S(1)}, pred[512,1056]{0,1:T(8,128)(4,1)}, u32[]{:S(2)}) copy-start(pred[512,1056]{0,1:T(8,128)(4,1)} %copy-done.4) | copy-start | bytes 1622020
  104.6 8.6 %slice-start = ((s8[8650752]{0:T(1024)(128)(4,1)}), s8[262144]{0:T(1024)(128)(4,1)S(1)}, s32[]{:S(2)}) async-start(s8[8650752]{0:T(1024)(128)(4,1)} %bitcast.103), calls=%async_computation.6 | async-start | bytes 524288
  105.7 7.5 %slice-start.1 = ((s8[8650752]{0:T(1024)(128)(4,1)}), s8[4194304]{0:T(1024)(128)(4,1)S(1)}, s32[]{:S(2)}) async-start(s8[8650752]{0:T(1024)(128)(4,1)} %bitcast.103), calls=%async_computation.7 | async-start | bytes 8388608
  105.7 7.5 %slice-start.2 = ((s8[8650752]{0:T(1024)(128)(4,1)}), s8[4194304]{0:T(1024)(128)(4,1)S(1)}, s32[]{:S(2)}) async-start(s8[8650752]{0:T(1024)(128)(4,1)} %bitcast.103), calls=%async_computation.8 | async-start | bytes 8388608
  105.7 7.5 %copy-start.6 = (pred[512,1056]{0,1:T(8,128)(4,1)S(1)}, pred[512,1056]{0,1:T(8,128)(4,1)}, u32[]{:S(2)}) copy-start(pred[512,1056]{0,1:T(8,128)(4,1)} %copy-done.4) | copy-start | bytes 1622020
  105.7 7.5 %copy-start.9 = (bf16[1024,1,384]{0,2,1:T(8,128)(2,1)S(1)}, bf16[1024,1,384]{0,2,1:T(8,128)(2,1)}, u32[]{:S(2)}) copy-start(bf16[1024,1,384]{0,2,1:T(8,128)(2,1)} %copy.53) | copy-start | bytes 2359300
  113.2 3.7 %copy-start.8 = (f32[2,512,4]{2,0,1:T(2,128)S(1)}, f32[2,512,4]{2,0,1:T(2,128)}, u32[]{:S(2)}) copy-start(f32[2,512,4]{2,0,1:T(2,128)} %copy.69) | copy-start | bytes 49156
  126.3 13.5 %all-to-all-start.2 = ((f32[16,1,256]{2,1,0:T(1,128)}), f32[16,1,256]{2,1,0:T(1,128)S(1)}, u32[]{:S(2)}, u32[]{:S(2)}) async-start(f32[16,1,256]{2,1,0:T(1,128)} %reshape.130), calls=%async_computation.2 | async-start | bytes 32768 | tf_op jit(solution)/shard_map/all_to_all | solution.py:78
  133.5 12.1 %copy-start.17 = (s32[1,64,1]{1,2,0:T(1,128)S(1)}, s32[1,64,1]{1,2,0:T(1,128)}, u32[]{:S(2)}) copy-start(s32[1,64,1]{1,2,0:T(1,128)} %param.19) | copy-start | bytes 772
  139.7 21.9 %all-to-all-start = ((f32[1,2,512,384]{3,1,0,2:T(2,128)}), f32[1,2,512,384]{3,1,0,2:T(2,128)}, u32[]{:S(2)}, u32[]{:S(2)}) async-start(f32[1,2,512,384]{3,1,0,2:T(2,128)} %maximum_bitcast_fusion), calls=%async_computation | async-start | bytes 3145728 | tf_op jit(solution)/shard_map/all_to_all | solution.py:79
  145.3 108.8 %reduce-scatter.4.cloned.1.call-start = ((), (), s32[]{:S(2)}) async-start(), calls=%async_computation.5 | async-start | bytes 884736
  161.6 2.2 copy-start.16
  161.6 1.9 copy-start.2
  163.3 45.9 %copy-start.18 = (f32[3072]{0:T(1024)S(1)}, f32[3072]{0:T(1024)}, u32[]{:S(2)}) copy-start(f32[3072]{0:T(1024)} %param.15) | copy-start | bytes 36868
  208.3 0.9 copy-start.3
Sparse Core Ops, SparseCore 0:
  219.1 34.9 reduce-scatter.3
where the time goes:
time: 264 us; the launch traced here: 263 us
  local copies, waits for them, and re-layouts  77.8 us (29%)
  blocking collectives  67.9 us (26%)
  waiting for transfers between devices  37.4 us (14%)
  matrix products  30.5 us (12%)
  starting transfers between devices  18.7 us (7%)
  other arithmetic  16.4 us (6%)
  between operations  13.7 us (5%)
    unnamed x2, waiting for transfers between devices  35.1 us
    all_gather x1, blocking collectives, per_device(): full_rows = lax.all_gather(arrived, 'tp', axis=1, tiled=True)  30 us
    all_gather x1, blocking collectives, per_device(): all_queries = lax.all_gather(queries, 'seq', axis=1, tiled=True)  24.4 us
    unnamed x52, local copies, waits for them, and re-layouts  16.3 us
    slice x3, local copies, waits for them, and re-layouts, slot_partial(): cached_slot[:, 1]  15.6 us
    all_to_all x1, blocking collectives, per_device(): lax.all_to_all(outgoing.reshape(owner_count, slot_cap, width_local), ('re...  13.5 us
    dot_general x2, matrix products, block_stats(): jnp.einsum('qhd,khd->qhk', query_heads, key_heads, preferred_element_type...  11.9 us
    dot_general x2, matrix products, block_stats(): jnp.einsum('qhk,khd->qhd', weights.astype(jnp.bfloat16), value_heads, pre...  11.2 us
  transfers between devices with their start and end apart: 4, of which 2 were waited for; matrix products, arithmetic and copies ran while one was open for 22% of the time, Pallas kernels for 0%

commit v1 on v0

--- a/solution.py
+++ b/solution.py
@@ -74,7 +74,12 @@
     row_total = jnp.stack([partial_item[1] for partial_item in partials])
     weighted = jnp.stack([partial_item[2] for partial_item in partials])
     pieces = (
-        lax.all_to_all(row_peak[None], "seq", split_axis=2, concat_axis=0, tiled=True),
+        jnp.concatenate(
+            lax.all_to_all(
+                jnp.stack(jnp.split(row_peak[None], lax.axis_size("seq"), axis=2)), "seq", 0, 0
+            ),
+            axis=0,
+        ),
         lax.all_to_all(row_total[None], "seq", split_axis=2, concat_axis=0, tiled=True),
         lax.all_to_all(weighted[None], "seq", split_axis=2, concat_axis=0, tiled=True),
     )

time: 264 us -> 258 us (0.977)
  local copies, waits for them, and re-layouts: 77.8 us -> 71.4 us
    unnamed x52 -> x66, local copies, waits for them, and re-layouts: 16.3 us -> 12.1 us
  transfers between devices with their start and end apart: 4 -> 4, of which waited for: 2 -> 3; matrix products, arithmetic and copies ran while one was open for 22% -> 22% of each run, Pallas kernels for 0% -> 0%
where the time goes in v1:
time: 258 us; the launch traced here: 257 us
  local copies, waits for them, and re-layouts  71.4 us (28%)
  blocking collectives  66.5 us (26%)
  waiting for transfers between devices  39.6 us (15%)
  matrix products  30.5 us (12%)
  starting transfers between devices  18.7 us (7%)
  other arithmetic  16.4 us (6%)
  between operations  13.8 us (5%)
    unnamed x2, waiting for transfers between devices  35.1 us
    all_gather x1, blocking collectives, per_device(): full_rows = lax.all_gather(arrived, 'tp', axis=1, tiled=True)  30 us
    all_gather x1, blocking collectives, per_device(): all_queries = lax.all_gather(queries, 'seq', axis=1, tiled=True)  24.4 us
    slice x3, local copies, waits for them, and re-layouts, slot_partial(): cached_slot[:, 1]  15.6 us
    unnamed x66, local copies, waits for them, and re-layouts  12.1 us
    all_to_all x1, blocking collectives, per_device(): lax.all_to_all(outgoing.reshape(owner_count, slot_cap, width_local), ('re...  12.1 us
    dot_general x2, matrix products, block_stats(): jnp.einsum('qhd,khd->qhk', query_heads, key_heads, preferred_element_type...  11.9 us
    dot_general x2, matrix products, block_stats(): jnp.einsum('qhk,khd->qhd', weights.astype(jnp.bfloat16), value_heads, pre...  11.2 us
  transfers between devices with their start and end apart: 4, of which 3 were waited for; matrix products, arithmetic and copies ran while one was open for 22% of the time, Pallas kernels for 0%

profile of v1, /device:TPU:2, one launch (start us, length us, event | category | flops | bytes accessed | tf_op | source)
XLA Modules:
  0.0 257.0 jit_solution(1888843541305301346)
XLA Ops:
  6.5 1.4 fusion.65
  8.0 1.3 fusion.45
  10.5 0.9 slice_bitcast_fusion.3
  11.4 0.8 fusion.63
  13.7 24.4 %all_gather.6 = bf16[2,512,384]{2,1,0:T(8,128)(2,1)S(1)} all-gather(bf16[2,32,384]{2,1,0:T(8,128)(2,1)} %param.10), channel_id=1, replica_groups=mesh['req'=2,'seq'=16,'tp'=8] {'seq'}, dimensions={1}, use_global_device_ids=true | all-gather | bytes 835584 | tf_op jit(solution)/shard_map/all_gather | solution.py:62
  38.1 0.8 fusion.62
  38.9 1.9 copy.71
  40.8 0.9 copy.76
  41.8 3.9 %slice_bitcast_fusion.1 = (bf16[1024,2,384]{2,1,0:T(2,128)(2,1)S(1)}, bf16[1024,2,384]{2,1,0:T(2,128)(2,1)S(1)}) fusion(bf16[2,1024,2,384]{3,2,1,0:T(2,128)(2,1)} %param.12), kind=kLoop, calls=%fused_computation.26 | loop fusion | bytes 6291456 | tf_op jit(solution)/shard_map/squeeze | solution.py:66
  45.6 6.3 %fusion.60 = (bf16[1024,1,384]{2,1,0:T(2,128)(2,1)}, bf16[1024,1,384]{2,1,0:T(2,128)(2,1)}, bf16[1024,1,384]{2,1,0:T(2,128)(2,1)}, bf16[1024,1,384]{2,1,0:T(2,128)(2,1)}) fusion(bf16[1024,2,384]{2,1,0:T(2,128)(2,1)S(1)} %get-tuple-element.7, bf16[1024,2,384]{2,1,0:T(2,128)(2,1)S(1)} %get-tuple-element.8), kind=kLoop, calls=%fused_computation.117 | loop fusion | bytes 6291456 | tf_op jit(solution)/shard_map/slice | solution.py:42
  51.9 4.7 %copy.69 = bf16[1024,1,384]{0,2,1:T(8,128)(2,1)} copy(bf16[1024,1,384]{2,1,0:T(2,128)(2,1)} %get-tuple-element.10) | data formatting | bytes 1572864 | tf_op jit(solution)/shard_map/slice | solution.py:39
  56.6 4.7 %copy.74 = bf16[1024,1,384]{0,2,1:T(8,128)(2,1)} copy(bf16[1024,1,384]{2,1,0:T(2,128)(2,1)} %get-tuple-element.33) | data formatting | bytes 1572864 | tf_op jit(solution)/shard_map/slice | solution.py:39
  61.3 1.8 pad_add_fusion.1
  63.2 6.7 %fusion.1 = (f32[512,4]{0,1:T(4,128)S(1)}, f32[4,1056,512]{2,1,0:T(8,128)}) fusion(pred[512,1056]{0,1:T(8,128)(4,1)S(1)} %get-tuple-element.22, bf16[512,4,96]{0,2,1:T(8,128)(2,1)S(1)} %bitcast.176, bf16[32,4,96]{0,2,1:T(8,128)(2,1)} %bitcast.178, bf16[1024,4,96]{0,2,1:T(8,128)(2,1)} %bitcast.173), kind=kOutput, calls=%fused_computation.6 | convolution fusion | flops 423344128 | bytes 10403840 | tf_op jit(solution)/shard_map/qhd,khd->qhk/dot_general | solution.py:11
  69.9 5.2 %fusion = (f32[512,4]{0,1:T(4,128)S(1)}, f32[4,1056,512]{2,1,0:T(8,128)}) fusion(pred[512,1056]{0,1:T(8,128)(4,1)S(1)} %get-tuple-element.21, bf16[512,4,96]{0,2,1:T(8,128)(2,1)S(1)} %bitcast.175, bf16[32,4,96]{0,2,1:T(8,128)(2,1)S(1)} %bitcast.177, bf16[1024,4,96]{0,2,1:T(8,128)(2,1)S(1)} %bitcast.171), kind=kOutput, calls=%fused_computation.5 | convolution fusion | flops 423344128 | bytes 10403840 | tf_op jit(solution)/shard_map/qhd,khd->qhk/dot_general | solution.py:11
  76.8 5.7 %all-to-all-start.1 = ((f32[16,1,256]{2,1,0:T(1,128)}), f32[16,1,256]{2,1,0:T(1,128)S(1)}, u32[]{:S(2)}, u32[]{:S(2)}) async-start(f32[16,1,256]{2,1,0:T(1,128)} %reshape.132), calls=%async_computation.1 | async-start | bytes 32768 | tf_op jit(solution)/shard_map/all_to_all | solution.py:78
  82.6 0.8 copy.73
  83.4 4.7 %copy.67 = bf16[1024,1,384]{0,2,1:T(8,128)(2,1)} copy(bf16[1024,1,384]{2,1,0:T(2,128)(2,1)} %get-tuple-element.9) | data formatting | bytes 1572864 | tf_op jit(solution)/shard_map/slice | solution.py:42
  88.0 4.7 %copy.72 = bf16[1024,1,384]{0,2,1:T(8,128)(2,1)} copy(bf16[1024,1,384]{2,1,0:T(2,128)(2,1)} %get-tuple-element.34) | data formatting | bytes 1572864 | tf_op jit(solution)/shard_map/slice | solution.py:42
  92.7 4.8 %fusion.4 = f32[512,4]{0,1:T(4,128)S(1)} fusion(f32[4,1056,512]{2,1,0:T(8,128)} %get-tuple-element.26, f32[512,4]{0,1:T(4,128)S(1)} %get-tuple-element.25, pred[512,1056]{0,1:T(8,128)(4,1)} %copy-done.7), kind=kLoop, calls=%fused_computation.9 | loop fusion | flops 10811392 | bytes 9207808 | tf_op jit(solution)/shard_map/reduce_sum | solution.py:18
  97.6 1.3 copy-done.1
  98.9 2.2 fusion.2
  101.1 1.0 copy.82
  102.2 7.5 %fusion.6 = f32[4,96,512]{2,1,0:T(8,128)} fusion(f32[4,1056,512]{2,1,0:T(8,128)} %get-tuple-element.26, f32[512,4]{0,1:T(4,128)S(1)} %get-tuple-element.25, pred[512,1056]{0,1:T(8,128)(4,1)} %copy-done.7, bf16[32,4,96]{0,2,1:T(8,128)(2,1)} %bitcast.180, bf16[1024,4,96]{0,2,1:T(8,128)(2,1)} %bitcast.172), kind=kOutput, calls=%fused_computation.11 | convolution fusion | flops 427671552 | bytes 10797056 | tf_op jit(solution)/shard_map/qhk,khd->qhd/dot_general | solution.py:19
  109.7 3.7 %fusion.8 = f32[4,96,512]{2,1,0:T(8,128)} fusion(f32[4,1056,512]{2,1,0:T(8,128)S(1)} %bitcast.164, f32[512,4]{0,1:T(4,128)S(1)} %get-tuple-element.27, pred[512,1056]{0,1:T(8,128)(4,1)S(1)} %copy-done.6, bf16[32,4,96]{0,2,1:T(8,128)(2,1)S(1)} %bitcast.179, bf16[1024,4,96]{0,2,1:T(8,128)(2,1)S(1)} %bitcast.170), kind=kOutput, calls=%fused_computation.12 | convolution fusion | flops 427671552 | bytes 10797056 | tf_op jit(solution)/shard_map/qhk,khd->qhd/dot_general | solution.py:19
  113.4 0.8 bitcast_bitcast_fusion
  114.3 3.1 %copy.78 = f32[1,512,384]{2,0,1:T(1,128)} copy(f32[1,512,384]{1,2,0:T(8,128)} %bitcast.168) | data formatting | bytes 1572864 | tf_op jit(solution)/shard_map/stack;reshape | solution.py:75
  117.3 3.0 %copy.77 = f32[1,512,384]{2,0,1:T(1,128)} copy(f32[1,512,384]{1,2,0:T(8,128)} %bitcast.169) | data formatting | bytes 1572864 | tf_op jit(solution)/shard_map/stack;reshape | solution.py:75
  120.4 2.4 reshape.134
  122.7 7.2 %all-to-all-start.2 = ((f32[16,1,256]{2,1,0:T(1,128)}), f32[16,1,256]{2,1,0:T(1,128)S(1)}, u32[]{:S(2)}, u32[]{:S(2)}) async-start(f32[16,1,256]{2,1,0:T(1,128)} %reshape.134), calls=%async_computation.2 | async-start | bytes 32768 | tf_op jit(solution)/shard_map/all_to_all | solution.py:83
  130.0 3.9 %maximum_bitcast_fusion = f32[1,2,512,384]{3,1,0,2:T(2,128)} fusion(f32[1,512,384]{2,0,1:T(1,128)} %copy.78, f32[1,512,384]{2,0,1:T(1,128)} %copy.77), kind=kLoop, calls=%fused_computation.23 | loop fusion | flops 393216 | bytes 3145728 | tf_op jit(solution)/shard_map/broadcast_in_dim | solution.py:84
  133.9 2.3 all-to-all-done.2
  136.2 5.6 %all-to-all-start = ((f32[1,2,512,384]{3,1,0,2:T(2,128)}), f32[1,2,512,384]{3,1,0,2:T(2,128)}, u32[]{:S(2)}, u32[]{:S(2)}) async-start(f32[1,2,512,384]{3,1,0,2:T(2,128)} %maximum_bitcast_fusion), calls=%async_computation | async-start | bytes 3145728 | tf_op jit(solution)/shard_map/all_to_all | solution.py:84
  144.4 1.6 reshape.135
  146.0 1.3 copy.85
  147.8 1.1 copy.81
  148.9 3.2 %mul.89 = f32[16,2,32,4,96]{4,3,2,0,1:T(4,128)} broadcast(f32[16,2,32,4]{3,2,0,1:T(8,128)} %copy.81), dimensions={0,1,2,3} | broadcast | bytes 1589248 | tf_op jit(solution)/shard_map/mul | solution.py:91
  152.1 3.2 %mul.90 = f32[16,1,2,32,384]{4,3,0,2,1:T(8,128)} reshape(f32[16,2,32,4,96]{4,3,2,0,1:T(4,128)} %mul.89) | data formatting | bytes 3145728 | tf_op jit(solution)/shard_map/mul | solution.py:91
  155.3 2.3 all-to-all-done
  157.5 1.6 copy.79
  159.7 0.9 scatter_custom_fusion
  160.6 12.1 %all_to_all.43 = bf16[32,4,384]{2,1,0:T(4,128)(2,1)S(1)} all-to-all(bf16[32,4,384]{2,1,0:T(4,128)(2,1)S(1)} %reshape.115), channel_id=1, replica_groups=mesh['req'=2,'seq'=16,'tp'=8] {'req','seq'}, dimensions={0} | all-to-all | bytes 196608 | tf_op jit(solution)/shard_map/all_to_all | solution.py:111
  172.7 30.0 %all_gather.7 = bf16[128,3072]{1,0:T(8,128)(2,1)S(1)} all-gather(bf16[128,384]{1,0:T(8,128)(2,1)S(1)} %reshape.116), channel_id=1, replica_groups=mesh['req'=2,'seq'=16,'tp'=8] {'tp'}, dimensions={1}, use_global_device_ids=true | all-gather | bytes 884736 | tf_op jit(solution)/shard_map/all_gather | solution.py:119
  203.7 3.2 %fusion.37 = f32[128,512]{1,0:T(8,128)} fusion(bf16[3072,512]{1,0:T(8,128)(2,1)} %param.16, bf16[128,3072]{1,0:T(8,128)(2,1)S(1)} %all_gather.7, f32[3072]{0:T(1024)S(1)} %copy-done.18, f32[128]{0:T(128)S(1)} %add_rsqrt_fusion), kind=kOutput, calls=%fused_computation.48 | convolution fusion | flops 404226048 | bytes 4207104 | tf_op jit(solution)/shard_map/dot_general | solution.py:121
  206.9 4.2 %convolution_convert_fusion = bf16[128,3072]{1,0:T(8,128)(2,1)} fusion(bf16[512,3072]{1,0:T(8,128)(2,1)S(1)} %copy-done, bf16[3072,512]{1,0:T(8,128)(2,1)} %param.17, f32[128,512]{1,0:T(8,128)} %fusion.37, bf16[128,3072]{1,0:T(8,128)(2,1)} %copy-done.3, f32[3072]{0:T(1024)S(1)} %copy-done.18, f32[128]{0:T(128)S(1)} %add_rsqrt_fusion), kind=kOutput, calls=%fused_computation.15 | convolution fusion | flops 807665664 | bytes 8139264 | tf_op jit(solution)/shard_map/dot_general | solution.py:124
  211.1 2.3 copy.86
  213.4 35.0 %reduce-scatter.4.cloned.1.call-done = bf16[384,128]{1,0:T(8,128)(2,1)} async-done(((bf16[3072,128]{1,0:T(8,128)(2,1)}), bf16[384,128]{1,0:T(8,128)(2,1)}) %reduce-scatter.4.cloned.1.call-update) | async-done | bytes 98320
  248.4 1.0 copy.87
  (94 shorter events, 10.0 us)
Async XLA Ops:
  6.5 200.3 %copy-start = (bf16[512,3072]{1,0:T(8,128)(2,1)S(1)}, bf16[512,3072]{1,0:T(8,128)(2,1)}, u32[]{:S(2)}) copy-start(bf16[512,3072]{1,0:T(8,128)(2,1)} %param.18) | copy-start | bytes 9437188
  51.9 11.2 %copy-start.12 = (bf16[1,512,384]{1,2,0:T(8,128)(2,1)S(1)}, bf16[1,512,384]{1,2,0:T(8,128)(2,1)}, u32[]{:S(2)}) copy-start(bf16[1,512,384]{1,2,0:T(8,128)(2,1)} %copy.76) | copy-start | bytes 1179652
  63.1 6.8 %copy-start.7 = (pred[512,1056]{0,1:T(8,128)(4,1)}, pred[512,1056]{0,1:T(8,128)(4,1)S(1)}, u32[]{:S(2)}) copy-start(pred[512,1056]{0,1:T(8,128)(4,1)S(1)} %get-tuple-element.22) | copy-start | bytes 1622020
  63.1 6.8 %copy-start.4 = (pred[512,1056]{0,1:T(8,128)(4,1)}, pred[512,1056]{0,1:T(8,128)(4,1)S(1)}, u32[]{:S(2)}) copy-start(pred[512,1056]{0,1:T(8,128)(4,1)S(1)} %get-tuple-element.21) | copy-start | bytes 1622020
  63.1 6.7 %copy-start.10 = (bf16[1024,1,384]{0,2,1:T(8,128)(2,1)S(1)}, bf16[1024,1,384]{0,2,1:T(8,128)(2,1)}, u32[]{:S(2)}) copy-start(bf16[1024,1,384]{0,2,1:T(8,128)(2,1)} %copy.69) | copy-start | bytes 2359300
  63.1 6.7 %copy-start.11 = (bf16[1,512,384]{1,2,0:T(8,128)(2,1)S(1)}, bf16[1,512,384]{1,2,0:T(8,128)(2,1)}, u32[]{:S(2)}) copy-start(bf16[1,512,384]{1,2,0:T(8,128)(2,1)} %copy.71) | copy-start | bytes 1179652
  63.1 6.7 %copy-start.15 = (bf16[32,1,384]{0,2,1:T(8,128)(2,1)S(1)}, bf16[32,1,384]{0,2,1:T(8,128)(2,1)}, u32[]{:S(2)}) copy-start(bf16[32,1,384]{0,2,1:T(8,128)(2,1)} %copy.70) | copy-start | bytes 73732
  69.9 12.6 %copy-start.14 = (bf16[32,1,384]{2,1,0:T(2,128)(2,1)S(1)}, bf16[32,1,384]{2,1,0:T(2,128)(2,1)}, u32[]{:S(2)}) copy-start(bf16[32,1,384]{2,1,0:T(2,128)(2,1)} %get-tuple-element.17) | copy-start | bytes 73732
  69.9 12.7 %copy-start.13 = (bf16[32,1,384]{2,1,0:T(2,128)(2,1)S(1)}, bf16[32,1,384]{2,1,0:T(2,128)(2,1)}, u32[]{:S(2)}) copy-start(bf16[32,1,384]{2,1,0:T(2,128)(2,1)} %get-tuple-element.32) | copy-start | bytes 73732
  76.8 45.9 %all-to-all-start.1 = ((f32[16,1,256]{2,1,0:T(1,128)}), f32[16,1,256]{2,1,0:T(1,128)S(1)}, u32[]{:S(2)}, u32[]{:S(2)}) async-start(f32[16,1,256]{2,1,0:T(1,128)} %reshape.132), calls=%async_computation.1 | async-start | bytes 32768 | tf_op jit(solution)/shard_map/all_to_all | solution.py:78
  92.7 6.1 %copy-start.1 = (f32[4,1056,512]{2,1,0:T(8,128)S(1)}, f32[4,1056,512]{2,1,0:T(8,128)}, u32[]{:S(2)}) copy-start(f32[4,1056,512]{2,1,0:T(8,128)} %get-tuple-element.28) | copy-start | bytes 25952260
  92.7 6.2 %copy-start.5 = (pred[512,1056]{0,1:T(8,128)(4,1)S(1)}, pred[512,1056]{0,1:T(8,128)(4,1)}, u32[]{:S(2)}) copy-start(pred[512,1056]{0,1:T(8,128)(4,1)} %copy-done.4) | copy-start | bytes 1622020
  101.1 8.6 %slice-start = ((s8[8650752]{0:T(1024)(128)(4,1)}), s8[262144]{0:T(1024)(128)(4,1)S(1)}, s32[]{:S(2)}) async-start(s8[8650752]{0:T(1024)(128)(4,1)} %bitcast.163), calls=%async_computation.6 | async-start | bytes 524288
  102.1 7.5 %slice-start.1 = ((s8[8650752]{0:T(1024)(128)(4,1)}), s8[4194304]{0:T(1024)(128)(4,1)S(1)}, s32[]{:S(2)}) async-start(s8[8650752]{0:T(1024)(128)(4,1)} %bitcast.163), calls=%async_computation.7 | async-start | bytes 8388608
  102.2 7.5 %slice-start.2 = ((s8[8650752]{0:T(1024)(128)(4,1)}), s8[4194304]{0:T(1024)(128)(4,1)S(1)}, s32[]{:S(2)}) async-start(s8[8650752]{0:T(1024)(128)(4,1)} %bitcast.163), calls=%async_computation.8 | async-start | bytes 8388608
  102.2 7.5 %copy-start.6 = (pred[512,1056]{0,1:T(8,128)(4,1)S(1)}, pred[512,1056]{0,1:T(8,128)(4,1)}, u32[]{:S(2)}) copy-start(pred[512,1056]{0,1:T(8,128)(4,1)} %copy-done.4) | copy-start | bytes 1622020
  102.2 7.5 %copy-start.9 = (bf16[1024,1,384]{0,2,1:T(8,128)(2,1)S(1)}, bf16[1024,1,384]{0,2,1:T(8,128)(2,1)}, u32[]{:S(2)}) copy-start(bf16[1024,1,384]{0,2,1:T(8,128)(2,1)} %copy.67) | copy-start | bytes 2359300
  109.7 3.7 %copy-start.8 = (f32[2,512,4]{2,0,1:T(2,128)S(1)}, f32[2,512,4]{2,0,1:T(2,128)}, u32[]{:S(2)}) copy-start(f32[2,512,4]{2,0,1:T(2,128)} %copy.82) | copy-start | bytes 49156
  122.7 13.5 %all-to-all-start.2 = ((f32[16,1,256]{2,1,0:T(1,128)}), f32[16,1,256]{2,1,0:T(1,128)S(1)}, u32[]{:S(2)}, u32[]{:S(2)}) async-start(f32[16,1,256]{2,1,0:T(1,128)} %reshape.134), calls=%async_computation.2 | async-start | bytes 32768 | tf_op jit(solution)/shard_map/all_to_all | solution.py:83
  130.0 12.1 %copy-start.17 = (s32[1,64,1]{1,2,0:T(1,128)S(1)}, s32[1,64,1]{1,2,0:T(1,128)}, u32[]{:S(2)}) copy-start(s32[1,64,1]{1,2,0:T(1,128)} %param.19) | copy-start | bytes 772
  136.2 21.3 %all-to-all-start = ((f32[1,2,512,384]{3,1,0,2:T(2,128)}), f32[1,2,512,384]{3,1,0,2:T(2,128)}, u32[]{:S(2)}, u32[]{:S(2)}) async-start(f32[1,2,512,384]{3,1,0,2:T(2,128)} %maximum_bitcast_fusion), calls=%async_computation | async-start | bytes 3145728 | tf_op jit(solution)/shard_map/all_to_all | solution.py:84
  141.8 106.7 %reduce-scatter.4.cloned.1.call-start = ((), (), s32[]{:S(2)}) async-start(), calls=%async_computation.5 | async-start | bytes 884736
  155.3 4.4 %copy-start.16 = (bf16[2,32,384]{2,1,0:T(8,128)(2,1)S(1)}, bf16[2,32,384]{2,1,0:T(8,128)(2,1)}, u32[]{:S(2)}) copy-start(bf16[2,32,384]{2,1,0:T(8,128)(2,1)} %param.14) | copy-start | bytes 147460
  157.5 1.9 copy-start.2
  159.2 44.5 %copy-start.18 = (f32[3072]{0:T(1024)S(1)}, f32[3072]{0:T(1024)}, u32[]{:S(2)}) copy-start(f32[3072]{0:T(1024)} %param.15) | copy-start | bytes 36868
  202.8 0.9 copy-start.3
Sparse Core Ops, SparseCore 0:
  213.5 34.8 reduce-scatter.3
